TPU v7x, 32 devices: a whole 2x2x4 slice. The times are simulated.
32 devices in a mesh: dev: 32 (over z, y, x, core).
Axes of the slice: x: 2, y: 2, z: 4, core: 2. Of those that a mesh axis runs over, the one named last changes fastest.
Arguments:
- tiles: bfloat16 [64, 128, 4096], P('dev'), may hold values from -6 to 6
- footprint: int32 [32, 21, 3], P('dev'), may hold values from 0 to 4032, as said below
- classes: int32 [32], P('dev'), may hold values from 0 to 15
- rotations: int32 [32], P('dev'), may hold values from 0 to 31
- references: bfloat16 [1024, 512], P('dev'), may hold values from -6 to 6
Outputs:
- scores: float32 [32, 512], P('dev')
- class_sums: float32 [1024, 512], P('dev')
Inputs may be any that keep to these rules, and one draw needn't show every extreme that they name: Rows and columns of a footprint lie inside the tile (64 and 4032 at most). Of the footprints of one device's particles at most 2 lie in the tiles held by any one device, and one device holds exactly 2 footprints of every device's particles.
All inputs are finite; a program needn't handle non-finite values.
Results may differ from a plain program's by a relative error of at most 0.0047.
Values may be sent and summed in bfloat16 or wider, within the bound.
No kernel may reach another device: no remote copies, remote signals or barrier semaphores. Data moves between devices by JAX's collectives and lax.ppermute only.
A program may use at most 128 MiB of HBM per device.

v0:
```python
import jax
import jax.numpy as jnp
from jax import lax
from jax.sharding import PartitionSpec as P

TILTS = 21
BOX = 64
CYCLES = 16
ROTS = 32
CLASSES = 16


def back_matrix(count):
    center = (BOX - 1) / 2.0
    tilt = jnp.arange(count, dtype=jnp.float32)[:, None, None, None]
    pixel = jnp.arange(BOX, dtype=jnp.float32)[None, :, None, None]
    xpos = jnp.arange(BOX, dtype=jnp.float32)[None, None, :, None]
    zpos = jnp.arange(BOX, dtype=jnp.float32)[None, None, None, :]
    theta = (-60.0 + 120.0 * tilt / (TILTS - 1)) * (jnp.pi / 180.0)
    place = (xpos - center) * jnp.cos(theta) + (zpos - center) * jnp.sin(theta) + center
    weight = jnp.maximum(0.0, 1.0 - jnp.abs(place - pixel))
    weight = jnp.where(tilt < TILTS, weight, 0.0) / TILTS
    return weight.reshape(count * BOX, BOX * BOX).astype(jnp.bfloat16)


def cyl_matrix():
    center = (BOX - 1) / 2.0
    xpos = jnp.arange(BOX, dtype=jnp.float32)[:, None, None, None]
    zpos = jnp.arange(BOX, dtype=jnp.float32)[None, :, None, None]
    angle = jnp.arange(ROTS, dtype=jnp.float32)[None, None, :, None] * (2.0 * jnp.pi / ROTS)
    radius = (jnp.arange(CYCLES, dtype=jnp.float32)[None, None, None, :] + 0.5) * (
        BOX / (2.0 * CYCLES)
    )
    wx = jnp.maximum(0.0, 1.0 - jnp.abs(xpos - center - radius * jnp.cos(angle)))
    wz = jnp.maximum(0.0, 1.0 - jnp.abs(zpos - center - radius * jnp.sin(angle)))
    return (wx * wz).reshape(BOX * BOX, ROTS * CYCLES).astype(jnp.bfloat16)


def shift_table():
    steps = jnp.arange(ROTS, dtype=jnp.int32)
    want = (steps[None, :, None] - steps[:, None, None]) % ROTS
    return (steps[None, None, :] == want).astype(jnp.float32)


def cut_many(tiles, items):
    flat = items.reshape(-1, 3)

    def cut(item):
        return lax.dynamic_slice(tiles, (item[0], item[1], item[2]), (1, BOX, BOX)).reshape(
            BOX * BOX
        )

    pieces = jax.vmap(cut)(flat)
    return pieces.reshape(items.shape[:-1] + (BOX * BOX,))


def per_device(tiles, footprint, classes, rotations, references):
    ndev = lax.axis_size("dev")
    count = footprint.shape[0]
    asks = count * TILTS
    cap = (2 * asks + ndev - 1) // ndev
    held = tiles.shape[0]
    flat = footprint.reshape(asks, 3)
    owner = flat[:, 0] // held
    local = flat[:, 0] - owner * held
    hits = (owner[:, None] == jnp.arange(ndev, dtype=jnp.int32)[None, :]).astype(jnp.int32)
    slot = jnp.sum((jnp.cumsum(hits, axis=0) - hits) * hits, axis=1)
    wanted = (
        jnp.zeros((ndev, cap, 3), jnp.int32)
        .at[owner, slot]
        .set(jnp.stack([local, flat[:, 1], flat[:, 2]], axis=-1))
    )
    patches_cut = cut_many(
        tiles, lax.all_to_all(wanted, "dev", split_axis=0, concat_axis=0, tiled=True)
    )
    arrived = lax.all_to_all(patches_cut, "dev", split_axis=0, concat_axis=0, tiled=True)
    patch = arrived[owner, slot].reshape(count, TILTS, BOX, BOX)
    padded = TILTS + TILTS % 2
    pmat = patch.transpose(0, 2, 1, 3)
    pmat = jnp.pad(pmat, ((0, 0), (0, 0), (0, padded - TILTS), (0, 0))).reshape(
        count * BOX, padded * BOX
    )
    volume = jnp.dot(pmat, back_matrix(padded), preferred_element_type=jnp.float32).astype(
        jnp.bfloat16
    )
    cyl = jnp.dot(volume, cyl_matrix(), preferred_element_type=jnp.float32).astype(jnp.bfloat16)
    cyl = cyl.reshape(count, BOX, ROTS * CYCLES)
    whole_refs = lax.all_gather(references, "dev", axis=0, tiled=True)
    ref_three = (
        whole_refs.reshape(CLASSES, BOX, ROTS, CYCLES)
        .transpose(0, 2, 1, 3)
        .reshape(CLASSES, ROTS, BOX * CYCLES)
    )
    ref_float = whole_refs.astype(jnp.float32).reshape(CLASSES, BOX * ROTS * CYCLES)
    ref_power = jnp.mean(ref_float * ref_float, axis=1)
    cyl_three = (
        cyl.reshape(count, BOX, ROTS, CYCLES)
        .transpose(0, 2, 1, 3)
        .reshape(count, ROTS, BOX * CYCLES)
    )
    corr = jnp.einsum("pfm,cgm->pcfg", cyl_three, ref_three, preferred_element_type=jnp.float32)
    raw = jnp.einsum("pcfg,kfg->pck", corr, shift_table(), precision=lax.Precision.HIGHEST)
    cyl_float = cyl.astype(jnp.float32)
    power = jnp.mean(cyl_float.reshape(count, -1) ** 2, axis=1)
    total = BOX * ROTS * CYCLES
    scores = raw / jnp.sqrt(
        total * (power[:, None, None] + 1e-06) * (ref_power[None, :, None] + 1e-06)
    )
    scores = scores.reshape(count, CLASSES * ROTS)
    columns = jnp.arange(ROTS * CYCLES, dtype=jnp.int32)
    index = (columns[None, :] + rotations[:, None] * CYCLES) % (ROTS * CYCLES)
    turned = jnp.take_along_axis(cyl, index[:, None, :], axis=2)
    member = (classes[:, None] == jnp.arange(CLASSES, dtype=jnp.int32)[None, :]).astype(
        jnp.bfloat16
    )
    owned = CLASSES * BOX // ndev
    placed = member[:, :, None, None] * turned[:, None, :, :]
    placed = placed.reshape(count, ndev, owned, ROTS * CYCLES)
    landed = lax.all_to_all(placed, "dev", split_axis=1, concat_axis=0, tiled=True)
    class_sums = jnp.sum(landed.astype(jnp.float32), axis=(0, 1))
    return (scores, class_sums)


def solution(mesh):
    in_specs = (P("dev", None, None), P("dev", None, None), P("dev"), P("dev"), P("dev", None))
    out_specs = (P("dev", None), P("dev", None))
    return jax.shard_map(
        per_device, mesh=mesh, in_specs=in_specs, out_specs=out_specs, check_vma=False
    )
```

profile of v0, /device:TPU:0, one launch (start us, length us, event | category | flops | bytes accessed | tf_op | source)
XLA Modules:
  0.0 373.9 jit_solution(16164082664645555117)
XLA Ops:
  8.9 4.0 %scatter_fusion = s32[32,2,3]{2,1,0:T(2,128)} fusion(s32[32,2,3]{2,1,0:T(2,128)} %broadcast_in_dim.14, s32[21]{0:T(128)S(1)} %get-tuple-element.20, s32[21,3]{1,0:T(8,128)S(1)} %copy.36), kind=kCustom, calls=%fused_computation.2 | custom fusion | bytes 924 | tf_op jit(solution)/shard_map/scatter | solution.py:71
  12.9 7.3 %all-to-all-start = ((s32[32,2,3]{2,1,0:T(2,128)}), s32[32,2,3]{2,1,0:T(2,128)S(1)}, u32[]{:S(2)}, u32[]{:S(2)}) async-start(s32[32,2,3]{2,1,0:T(2,128)} %scatter_fusion), calls=%async_computation | async-start | bytes 65536 | tf_op jit(solution)/shard_map/all_to_all | solution.py:74
  21.4 13.3 %multiply_convert_fusion = bf16[22,64,64,64]{3,2,1,0:T(8,128)(2,1)} fusion(f32[22,64,64]{2,1,0:T(8,128)S(1)} %add_add_fusion, pred[22]{0:T(512)(128)(4,1)S(1)} %iota_compare_fusion.3), kind=kLoop, calls=%fused_computation.5 | loop fusion | flops 40370176 | bytes 11894806 | tf_op jit(solution)/shard_map/convert_element_type | solution.py:23
  35.4 224.2 %while.1 = (s32[]{:T(128)}, bf16[2,128,4096]{2,1,0:T(8,128)(2,1)}, s32[64,3]{0,1:T(4,128)S(1)}, bf16[64,1,64,64]{3,2,1,0:T(8,128)(2,1)S(1)}, s32[]{:T(128)}) while((s32[]{:T(128)}, bf16[2,128,4096]{2,1,0:T(8,128)(2,1)}, s32[64,3]{0,1:T(4,128)S(1)}, bf16[64,1,64,64]{3,2,1,0:T(8,128)(2,1)S(1)}, s32[]{:T(128)}) %tuple.35), condition=%wide.while_cond, body=%wide.while_body.sunk | while | flops 2 | bytes 24705 | solution.py:49
  36.0 2.8 bitcast_dynamic-update-slice_fusion.2
  39.5 2.8 bitcast_dynamic-update-slice_fusion.2
  43.1 2.8 bitcast_dynamic-update-slice_fusion.2
  46.6 2.8 bitcast_dynamic-update-slice_fusion.2
  57.1 2.8 bitcast_dynamic-update-slice_fusion.2
  60.6 2.8 bitcast_dynamic-update-slice_fusion.2
  64.1 2.8 bitcast_dynamic-update-slice_fusion.2
  67.6 2.8 bitcast_dynamic-update-slice_fusion.2
  71.1 2.8 bitcast_dynamic-update-slice_fusion.2
  78.1 2.8 bitcast_dynamic-update-slice_fusion.2
  81.6 2.8 bitcast_dynamic-update-slice_fusion.2
  85.1 2.8 bitcast_dynamic-update-slice_fusion.2
  88.6 2.8 bitcast_dynamic-update-slice_fusion.2
  92.1 2.8 bitcast_dynamic-update-slice_fusion.2
  109.6 2.8 bitcast_dynamic-update-slice_fusion.2
  113.1 2.8 bitcast_dynamic-update-slice_fusion.2
  116.6 2.8 bitcast_dynamic-update-slice_fusion.2
  120.1 2.8 bitcast_dynamic-update-slice_fusion.2
  123.6 2.8 bitcast_dynamic-update-slice_fusion.2
  144.6 2.8 bitcast_dynamic-update-slice_fusion.2
  148.2 2.8 bitcast_dynamic-update-slice_fusion.2
  151.7 2.8 bitcast_dynamic-update-slice_fusion.2
  155.2 2.8 bitcast_dynamic-update-slice_fusion.2
  158.7 2.8 bitcast_dynamic-update-slice_fusion.2
  176.2 2.8 bitcast_dynamic-update-slice_fusion.2
  179.7 2.8 bitcast_dynamic-update-slice_fusion.2
  183.2 2.8 bitcast_dynamic-update-slice_fusion.2
  186.7 2.8 bitcast_dynamic-update-slice_fusion.2
  190.2 2.8 bitcast_dynamic-update-slice_fusion.2
  207.7 2.8 bitcast_dynamic-update-slice_fusion.2
  228.7 2.8 bitcast_dynamic-update-slice_fusion.2
  232.2 2.8 bitcast_dynamic-update-slice_fusion.2
  235.7 2.8 bitcast_dynamic-update-slice_fusion.2
  239.2 2.8 bitcast_dynamic-update-slice_fusion.2
  242.7 2.8 bitcast_dynamic-update-slice_fusion.2
  261.1 5.8 %all-to-all-start.1 = ((bf16[32,2,4096]{2,1,0:T(2,128)(2,1)}), bf16[32,2,4096]{2,1,0:T(2,128)(2,1)S(1)}, u32[]{:S(2)}, u32[]{:S(2)}) async-start(bf16[32,2,4096]{2,1,0:T(2,128)(2,1)} %reshape.573), calls=%async_computation.1 | async-start | bytes 1048576 | tf_op jit(solution)/shard_map/all_to_all | solution.py:76
  266.9 7.3 %multiply_convert_fusion.1 = bf16[64,64,32,16]{1,0,3,2:T(8,128)(2,1)} fusion(f32[64,32,16]{0,2,1:T(8,128)S(1)} %get-tuple-element.31, f32[64,32,16]{0,2,1:T(8,128)S(1)} %get-tuple-element.30), kind=kLoop, calls=%fused_computation.6 | loop fusion | flops 4194304 | bytes 4456448 | tf_op jit(solution)/shard_map/convert_element_type | solution.py:36
  274.3 12.1 %convert_element_type.63 = bf16[4096,512]{0,1:T(8,128)(2,1)} reshape(bf16[64,64,32,16]{1,0,3,2:T(8,128)(2,1)} %multiply_convert_fusion.1) | data formatting | bytes 8388608 | tf_op jit(solution)/shard_map/convert_element_type | solution.py:36
  286.3 30.6 %convert_element_type.60 = bf16[1408,4096]{1,0:T(8,128)(2,1)} reshape(bf16[22,64,64,64]{3,2,1,0:T(8,128)(2,1)} %multiply_convert_fusion) | data formatting | bytes 23068672 | tf_op jit(solution)/shard_map/convert_element_type | solution.py:23
  320.4 9.5 %multiply_reduce_fusion.1 = (f32[]{:T(128)}, bf16[64,512]{1,0:T(8,128)(2,1)S(1)}) fusion(bf16[4096,512]{0,1:T(8,128)(2,1)} %convert_element_type.63, bf16[64,1408]{1,0:T(8,128)(2,1)S(1)} %reshape.575, bf16[1408,4096]{1,0:T(8,128)(2,1)} %convert_element_type.60), kind=kOutput, calls=%fused_computation.23 | convolution fusion | flops 1007026176 | bytes 15974404 | tf_op jit(solution)/shard_map/dot_general | solution.py:86
  332.9 6.1 %all-to-all-start.2 = ((bf16[1,32,32,512]{3,2,0,1:T(8,128)(2,1)}), bf16[1,32,32,512]{3,2,0,1:T(8,128)(2,1)}, u32[]{:S(2)}, u32[]{:S(2)}) async-start(bf16[1,32,32,512]{3,2,0,1:T(8,128)(2,1)} %broadcast_multiply_fusion), calls=%async_computation.2 | async-start | bytes 2097152 | tf_op jit(solution)/shard_map/all_to_all | solution.py:119
  342.9 4.9 %copy.42 = bf16[16,32,64,16]{1,3,2,0:T(8,128)(2,1)} copy(bf16[16,32,64,16]{2,0,3,1:T(8,128)(2,1)S(1)} %bitcast.74) | data formatting | bytes 2097152 | tf_op jit(solution)/shard_map/transpose | solution.py:91
  349.5 3.0 convolution_bitcast_fusion
  353.7 11.4 %all-to-all-done.2 = bf16[1,32,32,512]{3,2,0,1:T(8,128)(2,1)} async-done(((bf16[1,32,32,512]{3,2,0,1:T(8,128)(2,1)}), bf16[1,32,32,512]{3,2,0,1:T(8,128)(2,1)}, u32[]{:S(2)}, u32[]{:S(2)}) %all-to-all-start.2) | async-done | bytes 1048608 | tf_op jit(solution)/shard_map/all_to_all | solution.py:119
  (218 shorter events, 142.6 us)
Async XLA Ops:
  12.9 22.1 %all-to-all-start = ((s32[32,2,3]{2,1,0:T(2,128)}), s32[32,2,3]{2,1,0:T(2,128)S(1)}, u32[]{:S(2)}, u32[]{:S(2)}) async-start(s32[32,2,3]{2,1,0:T(2,128)} %scatter_fusion), calls=%async_computation | async-start | bytes 65536 | tf_op jit(solution)/shard_map/all_to_all | solution.py:74
  20.2 319.8 %all-gather.2.cloned.1.call-start = ((), (), s32[]{:S(2)}) async-start(), calls=%async_computation.3 | async-start | bytes 1081344 | tf_op jit(solution)/shard_map/all_gather | solution.py:88
  261.1 57.3 %all-to-all-start.1 = ((bf16[32,2,4096]{2,1,0:T(2,128)(2,1)}), bf16[32,2,4096]{2,1,0:T(2,128)(2,1)S(1)}, u32[]{:S(2)}, u32[]{:S(2)}) async-start(bf16[32,2,4096]{2,1,0:T(2,128)(2,1)} %reshape.573), calls=%async_computation.1 | async-start | bytes 1048576 | tf_op jit(solution)/shard_map/all_to_all | solution.py:76
  332.9 32.2 %all-to-all-start.2 = ((bf16[1,32,32,512]{3,2,0,1:T(8,128)(2,1)}), bf16[1,32,32,512]{3,2,0,1:T(8,128)(2,1)}, u32[]{:S(2)}, u32[]{:S(2)}) async-start(bf16[1,32,32,512]{3,2,0,1:T(8,128)(2,1)} %broadcast_multiply_fusion), calls=%async_computation.2 | async-start | bytes 2097152 | tf_op jit(solution)/shard_map/all_to_all | solution.py:119
Sparse Core Ops, SparseCore 0:
  23.9 55.0 all-gather.1
where the time goes:
time: 381 us; the launch traced here: 374 us
  local copies, waits for them, and re-layouts  286 us (75%)
  other arithmetic  26.7 us (7%)
  starting transfers between devices  19.3 us (5%)
  between operations  16.2 us (4%)
  matrix products  13.1 us (3%)
  waiting for transfers between devices  12.1 us (3%)
    gather x192, local copies, waits for them, and re-layouts  223 us
    convert_element_type x1, local copies, waits for them, and re-layouts, back_matrix(): return weight.reshape(count * BOX, BOX * BOX).astype(jnp.bfloat16)  30.6 us
    convert_element_type x1, other arithmetic, back_matrix(): return weight.reshape(count * BOX, BOX * BOX).astype(jnp.bfloat16)  13.3 us
    convert_element_type x1, local copies, waits for them, and re-layouts, cyl_matrix(): return (wx * wz).reshape(BOX * BOX, ROTS * CYCLES).astype(jnp.bfloat16)  12.1 us
    all_to_all x1, waiting for transfers between devices, per_device(): lax.all_to_all(placed, 'dev', split_axis=1, concat_axis=0, tiled=True)  11.4 us
    dot_general x1, matrix products, per_device(): jnp.dot(volume, cyl_matrix(), preferred_element_type=jnp.float32)  9.51 us
  transfers between devices with their start and end apart: 4, of which 1 were waited for; matrix products, arithmetic and copies ran while one was open for 85% of the time, Pallas kernels for 0%

commit v1 on v0

--- a/solution.py
+++ b/solution.py
@@ -116,7 +116,10 @@
     owned = CLASSES * BOX // ndev
     placed = member[:, :, None, None] * turned[:, None, :, :]
     placed = placed.reshape(count, ndev, owned, ROTS * CYCLES)
-    landed = lax.all_to_all(placed, "dev", split_axis=1, concat_axis=0, tiled=True)
+    landed = jnp.concatenate(
+        lax.all_to_all(jnp.stack(jnp.split(placed, lax.axis_size("dev"), axis=1)), "dev", 0, 0),
+        axis=0,
+    )
     class_sums = jnp.sum(landed.astype(jnp.float32), axis=(0, 1))
     return (scores, class_sums)
 

time: 381 us -> 400 us (1.050)
  local copies, waits for them, and re-layouts: 286 us -> 305 us
    unnamed x4 -> x35, local copies, waits for them, and re-layouts: 0.9 us -> 19.6 us
  transfers between devices with their start and end apart: 4 -> 4, of which waited for: 1 -> 1; matrix products, arithmetic and copies ran while one was open for 85% -> 86% of each run, Pallas kernels for 0% -> 0%
where the time goes in v1:
time: 400 us; the launch traced here: 392 us
  local copies, waits for them, and re-layouts  305 us (76%)
  other arithmetic  25.7 us (6%)
  starting transfers between devices  19.1 us (5%)
  between operations  16.3 us (4%)
  matrix products  13.1 us (3%)
  waiting for transfers between devices  12.2 us (3%)
    gather x192, local copies, waits for them, and re-layouts  223 us
    convert_element_type x1, local copies, waits for them, and re-layouts, back_matrix(): return weight.reshape(count * BOX, BOX * BOX).astype(jnp.bfloat16)  30.6 us
    unnamed x35, local copies, waits for them, and re-layouts  19.6 us
    convert_element_type x1, other arithmetic, back_matrix(): return weight.reshape(count * BOX, BOX * BOX).astype(jnp.bfloat16)  13.3 us
    convert_element_type x1, local copies, waits for them, and re-layouts, cyl_matrix(): return (wx * wz).reshape(BOX * BOX, ROTS * CYCLES).astype(jnp.bfloat16)  12.1 us
    all_to_all x1, waiting for transfers between devices, per_device(): lax.all_to_all(jnp.stack(jnp.split(placed, lax.axis_size('dev'), axis=1))...  11.5 us
    dot_general x1, matrix products, per_device(): jnp.dot(volume, cyl_matrix(), preferred_element_type=jnp.float32)  9.51 us
  transfers between devices with their start and end apart: 4, of which 1 were waited for; matrix products, arithmetic and copies ran while one was open for 86% of the time, Pallas kernels for 0%

profile of v1, /device:TPU:0, one launch (start us, length us, event | category | flops | bytes accessed | tf_op | source)
XLA Modules:
  0.0 392.3 jit_solution(16512875470035786563)
XLA Ops:
  8.9 4.0 %scatter_fusion = s32[32,2,3]{2,1,0:T(2,128)} fusion(s32[32,2,3]{2,1,0:T(2,128)} %broadcast_in_dim.14, s32[21]{0:T(128)S(1)} %get-tuple-element.20, s32[21,3]{1,0:T(8,128)S(1)} %copy.24), kind=kCustom, calls=%fused_computation.2 | custom fusion | bytes 924 | tf_op jit(solution)/shard_map/scatter | solution.py:71
  12.9 7.3 %all-to-all-start = ((s32[32,2,3]{2,1,0:T(2,128)}), s32[32,2,3]{2,1,0:T(2,128)S(1)}, u32[]{:S(2)}, u32[]{:S(2)}) async-start(s32[32,2,3]{2,1,0:T(2,128)} %scatter_fusion), calls=%async_computation | async-start | bytes 65536 | tf_op jit(solution)/shard_map/all_to_all | solution.py:74
  21.4 13.3 %multiply_convert_fusion = bf16[22,64,64,64]{3,2,1,0:T(8,128)(2,1)} fusion(f32[22,64,64]{2,1,0:T(8,128)S(1)} %add_add_fusion, pred[22]{0:T(512)(128)(4,1)S(1)} %iota_compare_fusion.3), kind=kLoop, calls=%fused_computation.5 | loop fusion | flops 40370176 | bytes 11894806 | tf_op jit(solution)/shard_map/convert_element_type | solution.py:23
  35.4 224.2 %while.1 = (s32[]{:T(128)}, bf16[2,128,4096]{2,1,0:T(8,128)(2,1)}, s32[64,3]{0,1:T(4,128)S(1)}, bf16[64,1,64,64]{3,2,1,0:T(8,128)(2,1)S(1)}, s32[]{:T(128)}) while((s32[]{:T(128)}, bf16[2,128,4096]{2,1,0:T(8,128)(2,1)}, s32[64,3]{0,1:T(4,128)S(1)}, bf16[64,1,64,64]{3,2,1,0:T(8,128)(2,1)S(1)}, s32[]{:T(128)}) %tuple.35), condition=%wide.while_cond, body=%wide.while_body.sunk | while | flops 2 | bytes 24705 | solution.py:49
  36.0 2.8 bitcast_dynamic-update-slice_fusion.2
  39.5 2.8 bitcast_dynamic-update-slice_fusion.2
  43.1 2.8 bitcast_dynamic-update-slice_fusion.2
  46.6 2.8 bitcast_dynamic-update-slice_fusion.2
  57.1 2.8 bitcast_dynamic-update-slice_fusion.2
  60.6 2.8 bitcast_dynamic-update-slice_fusion.2
  64.1 2.8 bitcast_dynamic-update-slice_fusion.2
  67.6 2.8 bitcast_dynamic-update-slice_fusion.2
  71.1 2.8 bitcast_dynamic-update-slice_fusion.2
  78.1 2.8 bitcast_dynamic-update-slice_fusion.2
  81.6 2.8 bitcast_dynamic-update-slice_fusion.2
  85.1 2.8 bitcast_dynamic-update-slice_fusion.2
  88.6 2.8 bitcast_dynamic-update-slice_fusion.2
  92.1 2.8 bitcast_dynamic-update-slice_fusion.2
  109.6 2.8 bitcast_dynamic-update-slice_fusion.2
  113.1 2.8 bitcast_dynamic-update-slice_fusion.2
  116.6 2.8 bitcast_dynamic-update-slice_fusion.2
  120.1 2.8 bitcast_dynamic-update-slice_fusion.2
  123.6 2.8 bitcast_dynamic-update-slice_fusion.2
  144.6 2.8 bitcast_dynamic-update-slice_fusion.2
  148.2 2.8 bitcast_dynamic-update-slice_fusion.2
  151.7 2.8 bitcast_dynamic-update-slice_fusion.2
  155.2 2.8 bitcast_dynamic-update-slice_fusion.2
  158.7 2.8 bitcast_dynamic-update-slice_fusion.2
  176.2 2.8 bitcast_dynamic-update-slice_fusion.2
  179.7 2.8 bitcast_dynamic-update-slice_fusion.2
  183.2 2.8 bitcast_dynamic-update-slice_fusion.2
  186.7 2.8 bitcast_dynamic-update-slice_fusion.2
  190.2 2.8 bitcast_dynamic-update-slice_fusion.2
  207.7 2.8 bitcast_dynamic-update-slice_fusion.2
  228.7 2.8 bitcast_dynamic-update-slice_fusion.2
  232.2 2.8 bitcast_dynamic-update-slice_fusion.2
  235.7 2.8 bitcast_dynamic-update-slice_fusion.2
  239.2 2.8 bitcast_dynamic-update-slice_fusion.2
  242.7 2.8 bitcast_dynamic-update-slice_fusion.2
  261.1 5.8 %all-to-all-start.1 = ((bf16[32,2,4096]{2,1,0:T(2,128)(2,1)}), bf16[32,2,4096]{2,1,0:T(2,128)(2,1)S(1)}, u32[]{:S(2)}, u32[]{:S(2)}) async-start(bf16[32,2,4096]{2,1,0:T(2,128)(2,1)} %reshape.571), calls=%async_computation.1 | async-start | bytes 1048576 | tf_op jit(solution)/shard_map/all_to_all | solution.py:76
  266.9 7.3 %multiply_convert_fusion.1 = bf16[64,64,32,16]{1,0,3,2:T(8,128)(2,1)} fusion(f32[64,32,16]{0,2,1:T(8,128)S(1)} %get-tuple-element.31, f32[64,32,16]{0,2,1:T(8,128)S(1)} %get-tuple-element.30), kind=kLoop, calls=%fused_computation.6 | loop fusion | flops 4194304 | bytes 4456448 | tf_op jit(solution)/shard_map/convert_element_type | solution.py:36
  274.3 12.1 %convert_element_type.63 = bf16[4096,512]{0,1:T(8,128)(2,1)} reshape(bf16[64,64,32,16]{1,0,3,2:T(8,128)(2,1)} %multiply_convert_fusion.1) | data formatting | bytes 8388608 | tf_op jit(solution)/shard_map/convert_element_type | solution.py:36
  286.3 30.6 %convert_element_type.60 = bf16[1408,4096]{1,0:T(8,128)(2,1)} reshape(bf16[22,64,64,64]{3,2,1,0:T(8,128)(2,1)} %multiply_convert_fusion) | data formatting | bytes 23068672 | tf_op jit(solution)/shard_map/convert_element_type | solution.py:23
  320.4 9.5 %multiply_reduce_fusion.1 = (f32[]{:T(128)}, bf16[64,512]{1,0:T(8,128)(2,1)S(1)}) fusion(bf16[4096,512]{0,1:T(8,128)(2,1)} %convert_element_type.63, bf16[64,1408]{1,0:T(8,128)(2,1)S(1)} %reshape.573, bf16[1408,4096]{1,0:T(8,128)(2,1)} %convert_element_type.60), kind=kOutput, calls=%fused_computation.23 | convolution fusion | flops 1007026176 | bytes 15974404 | tf_op jit(solution)/shard_map/dot_general | solution.py:86
  351.3 6.0 %all-to-all-start.2 = ((bf16[32,1,1,32,512]{4,3,2,1,0:T(8,128)(2,1)}), bf16[32,1,1,32,512]{4,3,2,1,0:T(8,128)(2,1)}, u32[]{:S(2)}, u32[]{:S(2)}) async-start(bf16[32,1,1,32,512]{4,3,2,1,0:T(8,128)(2,1)} %constant_dynamic-update-slice_fusion), calls=%async_computation.2 | async-start | bytes 2097152 | tf_op jit(solution)/shard_map/all_to_all | solution.py:120
  361.1 4.9 %copy.30 = bf16[16,32,64,16]{1,3,2,0:T(8,128)(2,1)} copy(bf16[16,32,64,16]{2,0,3,1:T(8,128)(2,1)S(1)} %bitcast.202) | data formatting | bytes 2097152 | tf_op jit(solution)/shard_map/transpose | solution.py:91
  367.7 3.0 convolution_bitcast_fusion
  371.9 11.5 %all-to-all-done.2 = bf16[32,1,1,32,512]{4,3,2,1,0:T(8,128)(2,1)} async-done(((bf16[32,1,1,32,512]{4,3,2,1,0:T(8,128)(2,1)}), bf16[32,1,1,32,512]{4,3,2,1,0:T(8,128)(2,1)}, u32[]{:S(2)}, u32[]{:S(2)}) %all-to-all-start.2) | async-done | bytes 1048608 | tf_op jit(solution)/shard_map/all_to_all | solution.py:120
  (250 shorter events, 160.9 us)
Async XLA Ops:
  12.9 22.1 %all-to-all-start = ((s32[32,2,3]{2,1,0:T(2,128)}), s32[32,2,3]{2,1,0:T(2,128)S(1)}, u32[]{:S(2)}, u32[]{:S(2)}) async-start(s32[32,2,3]{2,1,0:T(2,128)} %scatter_fusion), calls=%async_computation | async-start | bytes 65536 | tf_op jit(solution)/shard_map/all_to_all | solution.py:74
  20.2 338.0 %all-gather.2.cloned.1.call-start = ((), (), s32[]{:S(2)}) async-start(), calls=%async_computation.3 | async-start | bytes 1081344 | tf_op jit(solution)/shard_map/all_gather | solution.py:88
  261.1 57.3 %all-to-all-start.1 = ((bf16[32,2,4096]{2,1,0:T(2,128)(2,1)}), bf16[32,2,4096]{2,1,0:T(2,128)(2,1)S(1)}, u32[]{:S(2)}, u32[]{:S(2)}) async-start(bf16[32,2,4096]{2,1,0:T(2,128)(2,1)} %reshape.571), calls=%async_computation.1 | async-start | bytes 1048576 | tf_op jit(solution)/shard_map/all_to_all | solution.py:76
  351.3 32.2 %all-to-all-start.2 = ((bf16[32,1,1,32,512]{4,3,2,1,0:T(8,128)(2,1)}), bf16[32,1,1,32,512]{4,3,2,1,0:T(8,128)(2,1)}, u32[]{:S(2)}, u32[]{:S(2)}) async-start(bf16[32,1,1,32,512]{4,3,2,1,0:T(8,128)(2,1)} %constant_dynamic-update-slice_fusion), calls=%async_computation.2 | async-start | bytes 2097152 | tf_op jit(solution)/shard_map/all_to_all | solution.py:120
Sparse Core Ops, SparseCore 0:
  23.9 55.0 all-gather.1
